TPU v7x, 512 devices: a whole 4x8x8 slice. The times are simulated.
512 devices in a mesh: ctx: 64 (over y_hi, x, z), head: 8 (over y_lo, core).
Axes of the slice: x: 4, y: 8 (y_hi: 2, y_lo: 4; y = y_hi * 4 + y_lo), z: 8, core: 2. Of those that a mesh axis runs over, the one named last changes fastest.
Arguments:
- q_self: bfloat16 [8192, 4096], P('ctx', 'head'), may hold values from -6 to 6
- k_self: bfloat16 [8192, 4096], P('ctx', 'head'), may hold values from -6 to 6
- v_self: bfloat16 [8192, 4096], P('ctx', 'head'), may hold values from -6 to 6
- q_cross: bfloat16 [8192, 4096], P('ctx', 'head'), may hold values from -6 to 6
- n_keys: bfloat16 [32768, 4096], P('ctx', 'head'), may hold values from -6 to 6
- n_values: bfloat16 [32768, 4096], P('ctx', 'head'), may hold values from -6 to 6
- d_cross: bfloat16 [8192, 4096], P('ctx', 'head'), may hold values from -16 to 16
Outputs:
- self_out: bfloat16 [8192, 4096], P('ctx', 'head')
- cross_out: bfloat16 [8192, 4096], P('ctx', 'head')
- d_query: bfloat16 [8192, 4096], P('ctx', 'head')
- d_keys: bfloat16 [32768, 4096], P('ctx', 'head')
- d_values: bfloat16 [32768, 4096], P('ctx', 'head')
All inputs are finite; a program needn't handle non-finite values.
Results may differ from a plain program's by a relative error of at most 0.012.
Values may be sent and summed in bfloat16 or wider, within the bound.
No kernel may reach another device: no remote copies, remote signals or barrier semaphores. Data moves between devices by JAX's collectives and lax.ppermute only.
A program may use at most 128 MiB of HBM per device.

v0:
```python
import math
import jax
import jax.numpy as jnp
from jax import lax
from jax.sharding import PartitionSpec as P

HD = 128
SPAN = 64


def from_behind(block, axis, distance):
    devices = range(lax.axis_size(axis))
    route = [(i - distance, i) for i in devices if i - distance in devices]
    return lax.ppermute(block, axis, route)


def attend_block(folded, keys_block, values_block, key_first, queries, positions):
    running_max, running_sum, accumulated = folded
    scores = jnp.einsum("rhd,khd->hrk", queries, keys_block, preferred_element_type=jnp.float32) * (
        1.0 / math.sqrt(HD)
    )
    key_positions = key_first + jnp.arange(keys_block.shape[0], dtype=jnp.int32)
    visible = (key_positions[None, :] <= positions[:, None])[None]
    masked = jnp.where(visible, scores, jnp.float32(-1e30))
    new_max = jnp.maximum(running_max, jnp.max(masked, axis=2))
    weights = jnp.where(visible, jnp.exp(masked - new_max[:, :, None]), jnp.float32(0.0))
    rescale = jnp.exp(running_max - new_max)
    new_sum = running_sum * rescale + jnp.sum(weights, axis=2)
    product = jnp.einsum(
        "hrk,khd->hrd",
        weights.astype(jnp.bfloat16),
        values_block,
        preferred_element_type=jnp.float32,
    )
    return (new_max, new_sum, accumulated * rescale[:, :, None] + product)


def self_attention(groups, keys_local, values_local):
    column_count = keys_local.shape[1]
    head_count = column_count // HD
    prepared = []
    for queries_flat, positions in groups:
        row_count = queries_flat.shape[0]
        prepared.append(
            (queries_flat.reshape(row_count, head_count, HD), positions, jnp.max(positions))
        )
    initial = tuple(
        (
            (
                jnp.full((head_count, entry[0].shape[0]), -1e30, jnp.float32),
                jnp.zeros((head_count, entry[0].shape[0]), jnp.float32),
                jnp.zeros((head_count, entry[0].shape[0], HD), jnp.float32),
            )
            for entry in prepared
        )
    )
    folded = initial
    keys_piece = lax.all_gather(keys_local, "ctx", axis=0, tiled=True)
    values_piece = lax.all_gather(values_local, "ctx", axis=0, tiled=True)
    piece_rows = keys_piece.shape[0]
    block_rows = 512
    block_count = piece_rows // block_rows
    key_blocks = keys_piece.reshape(block_count, block_rows, head_count, HD)
    value_blocks = values_piece.reshape(block_count, block_rows, head_count, HD)

    def visit(inner, items):
        keys_block, values_block, block_index = items
        key_first = block_index * block_rows
        updated = []
        for state, entry in zip(inner, prepared):
            queries, positions, last_position = entry

            def update(current, queries=queries, positions=positions):
                return attend_block(
                    current, keys_block, values_block, key_first, queries, positions
                )

            def unchanged(current):
                return current

            updated.append(lax.cond(key_first <= last_position, update, unchanged, state))
        return (tuple(updated), None)

    folded, unused = lax.scan(
        visit, folded, (key_blocks, value_blocks, jnp.arange(block_count, dtype=jnp.int32))
    )
    outputs = []
    for state in folded:
        running_max, running_sum, accumulated = state
        mixed = accumulated / running_sum[:, :, None]
        row_count = mixed.shape[1]
        outputs.append(
            mixed.transpose(1, 0, 2).reshape(row_count, column_count).astype(jnp.bfloat16)
        )
    return outputs


def cross_attention(q_cross, n_keys, n_values, d_cross):
    row_count, column_count = q_cross.shape
    head_count = column_count // HD
    lag_rows = SPAN - 1
    scale_factor = 1.0 / math.sqrt(HD)
    incoming = from_behind(q_cross[:lag_rows], "ctx", -1)
    shifted = jnp.concatenate([q_cross[lag_rows:], incoming], axis=0)
    span_count = row_count // SPAN
    neighbour_rows = n_keys.shape[0] // span_count
    queries = shifted.reshape(span_count, SPAN, head_count, HD)
    neighbour_keys = n_keys.reshape(span_count, neighbour_rows, head_count, HD)
    neighbour_values = n_values.reshape(span_count, neighbour_rows, head_count, HD)
    grad_rows = d_cross.reshape(span_count, SPAN, head_count, HD)
    scores = (
        jnp.einsum("crhd,ckhd->chrk", queries, neighbour_keys, preferred_element_type=jnp.float32)
        * scale_factor
    )
    row_max = jnp.max(scores, axis=3, keepdims=True)
    weights = jnp.exp(scores - row_max)
    probs = weights / jnp.sum(weights, axis=3, keepdims=True)
    probs_low = probs.astype(jnp.bfloat16)
    attended = jnp.einsum(
        "chrk,ckhd->crhd", probs_low, neighbour_values, preferred_element_type=jnp.float32
    )
    cross_out = attended.reshape(row_count, column_count).astype(jnp.bfloat16)
    grad_probs = jnp.einsum(
        "crhd,ckhd->chrk", grad_rows, neighbour_values, preferred_element_type=jnp.float32
    )
    centre = jnp.sum(grad_probs * probs, axis=3, keepdims=True)
    grad_scores = (probs * (grad_probs - centre) * scale_factor).astype(jnp.bfloat16)
    grad_source = jnp.einsum(
        "chrk,ckhd->crhd", grad_scores, neighbour_keys, preferred_element_type=jnp.float32
    )
    grad_source = grad_source.reshape(row_count, column_count).astype(jnp.bfloat16)
    grad_keys = jnp.einsum(
        "chrk,crhd->ckhd", grad_scores, queries, preferred_element_type=jnp.float32
    ).reshape(n_keys.shape)
    grad_values = jnp.einsum(
        "chrk,crhd->ckhd", probs_low, grad_rows, preferred_element_type=jnp.float32
    ).reshape(n_values.shape)
    carried = from_behind(grad_source[row_count - lag_rows :], "ctx", 1)
    d_query = jnp.concatenate([carried, grad_source[: row_count - lag_rows]], axis=0)
    squares = jnp.sum(grad_keys * grad_keys) + jnp.sum(grad_values * grad_values)
    overall = lax.psum(squares, ("ctx", "head"))
    element_count = 2.0 * grad_keys.size * lax.axis_size("ctx") * lax.axis_size("head")
    factor = lax.rsqrt(overall / element_count + 1e-06)
    d_keys = (grad_keys * factor).astype(jnp.bfloat16)
    d_values = (grad_values * factor).astype(jnp.bfloat16)
    return (cross_out, d_query, d_keys, d_values)


def body(q_self, k_self, v_self, q_cross, n_keys, n_values, d_cross):
    row_count = q_self.shape[0]
    device_index = lax.axis_index("ctx")
    first_row = device_index * row_count
    own_positions = first_row + jnp.arange(row_count, dtype=jnp.int32)
    self_out = self_attention([(q_self, own_positions)], k_self, v_self)[0]
    cross_out, d_query, d_keys, d_values = cross_attention(q_cross, n_keys, n_values, d_cross)
    return (self_out, cross_out, d_query, d_keys, d_values)


def solution(mesh):
    in_specs = (
        P("ctx", "head"),
        P("ctx", "head"),
        P("ctx", "head"),
        P("ctx", "head"),
        P("ctx", "head"),
        P("ctx", "head"),
        P("ctx", "head"),
    )
    out_specs = (
        P("ctx", "head"),
        P("ctx", "head"),
        P("ctx", "head"),
        P("ctx", "head"),
        P("ctx", "head"),
    )
    return jax.shard_map(body, mesh=mesh, in_specs=in_specs, out_specs=out_specs, check_vma=False)
```

profile of v0, /device:TPU:54, one launch (start us, length us, event | category | flops | bytes accessed | tf_op | source)
XLA Modules:
  0.0 502.9 jit_solution(6560523842506963549)
XLA Ops:
  9.5 11.2 %collective-permute-start = (bf16[63,512]{1,0:T(8,128)(2,1)S(1)}, bf16[63,512]{1,0:T(8,128)(2,1)S(1)}, u32[]{:S(2)}, u32[]{:S(2)}) collective-permute-start(bf16[63,512]{1,0:T(8,128)(2,1)S(1)} %slice.13), channel_id=1, source_target_pairs={{8,0},{16,8},{24,16},{32,24},{40,32},{48,40},{56,48},{64,56},{72,6... | collective-permute-start | bytes 193544 | tf_op jit(solution)/shard_map/ppermute | solution.py:14
  34.1 4.7 multiply_reduce_fusion.1
  41.9 143.9 %psum.7 = f32[]{:T(128)} all-reduce(f32[]{:T(128)S(6)} %add.41), channel_id=1, replica_groups=mesh['ctx'=64,'head'=8] {'ctx','head'}, use_global_device_ids=true, to_apply=%region_12.13 | all-reduce | flops 1 | bytes 8 | tf_op jit(solution)/shard_map/psum | solution.py:141
  191.8 12.7 %all-gather.3.cloned.1.call-done = bf16[8192,512]{1,0:T(8,128)(2,1)} async-done(((bf16[128,512]{1,0:T(8,128)(2,1)}), bf16[8192,512]{1,0:T(8,128)(2,1)}) %all-gather.3.cloned.1.call-update) | async-done | bytes 8388624 | tf_op jit(solution)/shard_map/all_gather | solution.py:58
  204.5 12.5 %reshape.91 = bf16[16,512,4,128]{3,2,1,0:T(4,128)(2,1)} reshape(bf16[8192,512]{1,0:T(8,128)(2,1)} %all-gather.3.cloned.1.call-done) | data formatting | bytes 16777216 | tf_op jit(solution)/shard_map/reshape | solution.py:63
  217.1 8.9 %copy.24 = bf16[16,512,4,128]{3,1,2,0:T(8,128)(2,1)} copy(bf16[16,512,4,128]{3,2,1,0:T(4,128)(2,1)} %reshape.91) | data formatting | bytes 16777216
  226.0 166.7 %all-gather.5.cloned.1.call-done = bf16[8192,512]{1,0:T(8,128)(2,1)} async-done(((bf16[128,512]{1,0:T(8,128)(2,1)}), bf16[8192,512]{1,0:T(8,128)(2,1)}) %all-gather.5.cloned.1.call-update) | async-done | bytes 8388624 | tf_op jit(solution)/shard_map/all_gather | solution.py:59
  392.7 12.5 %reshape.92 = bf16[16,512,4,128]{3,2,1,0:T(4,128)(2,1)} reshape(bf16[8192,512]{1,0:T(8,128)(2,1)} %all-gather.5.cloned.1.call-done) | data formatting | bytes 16777216 | tf_op jit(solution)/shard_map/reshape | solution.py:64
  405.2 8.9 %copy.26 = bf16[16,512,4,128]{3,1,2,0:T(8,128)(2,1)} copy(bf16[16,512,4,128]{3,2,1,0:T(4,128)(2,1)} %reshape.92) | data formatting | bytes 16777216
  414.1 81.2 %while.15 = (s32[]{:T(128)}, f32[4,128]{1,0:T(4,128)S(1)}, f32[4,128]{1,0:T(4,128)S(1)}, f32[4,128,128]{2,1,0:T(8,128)S(1)}, s32[16]{0:T(128)S(1)}, /*index=5*/s...) while((s32[]{:T(128)}, f32[4,128]{1,0:T(4,128)S(1)}, ...), condition=%wide.region_6.7_spmd.clone, body=%wide.region_1.6_spmd.clone.sunk | while | flops 136775296 | bytes 5152051 | solution.py:84
  416.0 3.3 conditional.3
  426.6 3.3 conditional.3
  431.9 3.3 conditional.3
  437.2 3.3 conditional.3
  442.4 3.3 conditional.3
  447.7 3.3 conditional.3
  453.0 3.3 conditional.3
  458.3 3.3 conditional.3
  463.6 3.3 conditional.3
  468.8 3.3 conditional.3
  474.1 3.3 conditional.3
  479.4 3.3 conditional.3
  484.7 3.3 conditional.3
  490.0 3.3 conditional.3
  (215 shorter events, 86.6 us)
Async XLA Ops:
  7.2 197.4 %all-gather.3.cloned.1.call-start = ((), (), s32[]{:S(2)}) async-start(), calls=%async_computation | async-start | bytes 8519680 | tf_op jit(solution)/shard_map/all_gather | solution.py:58
  7.9 384.8 %all-gather.5.cloned.1.call-start = ((), (), s32[]{:S(2)}) async-start(), calls=%async_computation.1 | async-start | bytes 8519680 | tf_op jit(solution)/shard_map/all_gather | solution.py:59
  9.5 17.6 %collective-permute-start = (bf16[63,512]{1,0:T(8,128)(2,1)S(1)}, bf16[63,512]{1,0:T(8,128)(2,1)S(1)}, u32[]{:S(2)}, u32[]{:S(2)}) collective-permute-start(bf16[63,512]{1,0:T(8,128)(2,1)S(1)} %slice.13), channel_id=1, source_target_pairs={{8,0},{16,8},{24,16},{32,24},{40,32},{48,40},{56,48},{64,56},{72,6... | collective-permute-start | bytes 193544 | tf_op jit(solution)/shard_map/ppermute | solution.py:14
  23.1 8.4 %copy-start.1 = (f32[2,4,64,256]{3,2,1,0:T(8,128)}, f32[2,4,64,256]{3,2,1,0:T(8,128)S(1)}, u32[]{:S(2)}) copy-start(f32[2,4,64,256]{3,2,1,0:T(8,128)S(1)} %fusion.34) | copy-start | bytes 1572868
  27.2 4.4 copy-start
  28.9 3.3 copy-start.2
  40.0 150.3 %collective-permute-start.1 = (bf16[63,512]{1,0:T(8,128)(2,1)}, bf16[63,512]{1,0:T(8,128)(2,1)}, u32[]{:S(2)}, u32[]{:S(2)}) collective-permute-start(bf16[63,512]{1,0:T(8,128)(2,1)} %slice.16), channel_id=1, source_target_pairs={{0,8},{8,16},{16,24},{24,32},{32,40},{40,48},{48,56},{56,64},{64,7... | collective-permute-start | bytes 193544 | tf_op jit(solution)/shard_map/ppermute | solution.py:14
Sparse Core Ops, SparseCore 0:
  12.5 192.0 all-gather.2
  209.1 183.5 all-gather.4
where the time goes:
time: 506 us; the launch traced here: 503 us
  waiting for transfers between devices  181 us (36%)
  blocking collectives  144 us (28%)
  local copies, waits for them, and re-layouts  63.2 us (12%)
  matrix products  54 us (11%)
  loops' own time  21.4 us (4%)
  between operations  16.1 us (3%)
  starting transfers between devices  13.2 us (3%)
  other arithmetic  10.2 us (2%)
    all_gather x1, waiting for transfers between devices, self_attention(): values_piece = lax.all_gather(values_local, 'ctx', axis=0, tiled=True)  167 us
    psum x1, blocking collectives, cross_attention(): overall = lax.psum(squares, ('ctx', 'head'))  144 us
    dot_general x15, matrix products, attend_block(): jnp.einsum('hrk,khd->hrd', weights.astype(jnp.bfloat16), values_block, pr...  22.8 us
    dot_general x15, matrix products, attend_block(): jnp.einsum('rhd,khd->hrk', queries, keys_block, preferred_element_type=jn...  20.6 us
    another operation x1, loops' own time, self_attention(): lax.scan(visit, folded, (key_blocks, value_blocks, jnp.arange(block_count...  20.6 us
    unnamed x12, local copies, waits for them, and re-layouts  19.6 us
    ppermute x2, starting transfers between devices, from_behind(): return lax.ppermute(block, axis, route)  13.1 us
    all_gather x1, waiting for transfers between devices, self_attention(): keys_piece = lax.all_gather(keys_local, 'ctx', axis=0, tiled=True)  12.7 us
  transfers between devices with their start and end apart: 4, of which 2 were waited for; matrix products, arithmetic and copies ran while one was open for 9% of the time, Pallas kernels for 0%

commit v1 on v0

--- a/solution.py
+++ b/solution.py
@@ -55,7 +55,9 @@
         )
     )
     folded = initial
-    keys_piece = lax.all_gather(keys_local, "ctx", axis=0, tiled=True)
+    keys_piece = jnp.concatenate(
+        lax.all_to_all(jnp.stack([keys_local] * lax.axis_size("ctx")), "ctx", 0, 0), axis=0
+    )
     values_piece = lax.all_gather(values_local, "ctx", axis=0, tiled=True)
     piece_rows = keys_piece.shape[0]
     block_rows = 512

time: 506 us -> 587 us (1.16)
  the two profiles are of different devices: /device:TPU:54 before, /device:TPU:310 now
where the time goes in v1:
time: 587 us; the launch traced here: 584 us
  blocking collectives  200 us (34%)
  waiting for transfers between devices  175 us (30%)
  local copies, waits for them, and re-layouts  83 us (14%)
  matrix products  56.9 us (10%)
  loops' own time  22.2 us (4%)
  starting transfers between devices  20 us (3%)
  between operations  16.3 us (3%)
  other arithmetic  10.6 us (2%)
    psum x1, blocking collectives, cross_attention(): overall = lax.psum(squares, ('ctx', 'head'))  200 us
    ppermute x2, waiting for transfers between devices, from_behind(): return lax.ppermute(block, axis, route)  174 us
    unnamed x23, local copies, waits for them, and re-layouts  25.5 us
    dot_general x16, matrix products, attend_block(): jnp.einsum('hrk,khd->hrd', weights.astype(jnp.bfloat16), values_block, pr...  24.3 us
    dot_general x16, matrix products, attend_block(): jnp.einsum('rhd,khd->hrk', queries, keys_block, preferred_element_type=jn...  22 us
    another operation x1, loops' own time, self_attention(): lax.scan(visit, folded, (key_blocks, value_blocks, jnp.arange(block_count...  21.3 us
    all_to_all x1, starting transfers between devices, self_attention(): lax.all_to_all(jnp.stack([keys_local] * lax.axis_size('ctx')), 'ctx', 0, 0)  15.6 us
    another operation x1, local copies, waits for them, and re-layouts, self_attention(): key_blocks = keys_piece.reshape(block_count, block_rows, head_count, HD)  14 us
  transfers between devices with their start and end apart: 4, of which 1 were waited for; matrix products, arithmetic and copies ran while one was open for 10% of the time, Pallas kernels for 0%

profile of v1, /device:TPU:310, one launch (start us, length us, event | category | flops | bytes accessed | tf_op | source)
XLA Modules:
  0.0 583.9 jit_solution(6328420917868201979)
XLA Ops:
  8.2 5.2 stack.2
  13.5 15.6 %all-to-all-start = ((bf16[64,128,512]{1,2,0:T(8,128)(2,1)}), bf16[64,128,512]{1,2,0:T(8,128)(2,1)}, u32[]{:S(2)}, u32[]{:S(2)}) async-start(bf16[64,128,512]{1,2,0:T(8,128)(2,1)} %stack.2), calls=%async_computation | async-start | bytes 16777216 | tf_op jit(solution)/shard_map/all_to_all | solution.py:59
  33.9 174.2 %collective-permute-done = bf16[63,512]{1,0:T(8,128)(2,1)S(1)} collective-permute-done((bf16[63,512]{1,0:T(8,128)(2,1)S(1)}, bf16[63,512]{1,0:T(8,128)(2,1)S(1)}, u32[]{:S(2)}, u32[]{:S(2)}) %collective-permute-start) | collective-permute-done | bytes 64544 | tf_op jit(solution)/shard_map/ppermute | solution.py:14
  215.1 4.8 multiply_reduce_fusion.1
  223.1 199.9 %psum.7 = f32[]{:T(128)} all-reduce(f32[]{:T(128)S(6)} %add.41), channel_id=1, replica_groups=mesh['ctx'=64,'head'=8] {'ctx','head'}, use_global_device_ids=true, to_apply=%region_12.13 | all-reduce | flops 1 | bytes 8 | tf_op jit(solution)/shard_map/psum | solution.py:143
  429.0 12.0 %copy.42 = bf16[64,128,512]{1,0,2:T(8,128)(2,1)} copy(bf16[64,128,512]{1,2,0:T(8,128)(2,1)} %all-to-all-done) | data formatting | bytes 16777216 | tf_op jit(solution)/shard_map/all_to_all | solution.py:59
  441.0 14.0 %reshape_reshape.3 = bf16[16,512,4,128]{1,0,3,2:T(8,128)(2,1)} reshape(bf16[64,128,512]{1,0,2:T(8,128)(2,1)} %copy.42) | data formatting | bytes 16777216 | tf_op jit(solution)/shard_map/reshape;reshape | solution.py:65
  454.9 14.6 %copy.45 = bf16[16,512,4,128]{3,1,2,0:T(8,128)(2,1)} copy(bf16[16,512,4,128]{1,0,3,2:T(8,128)(2,1)} %reshape_reshape.3) | data formatting | bytes 16777216
  469.6 12.5 %reshape.89 = bf16[16,512,4,128]{3,2,1,0:T(4,128)(2,1)} reshape(bf16[8192,512]{1,0:T(8,128)(2,1)} %all-gather.2.cloned.1.call-done) | data formatting | bytes 16777216 | tf_op jit(solution)/shard_map/reshape | solution.py:66
  482.1 8.9 %copy.47 = bf16[16,512,4,128]{3,1,2,0:T(8,128)(2,1)} copy(bf16[16,512,4,128]{3,2,1,0:T(4,128)(2,1)} %reshape.89) | data formatting | bytes 16777216
  491.0 85.2 %while.15 = (s32[]{:T(128)}, f32[4,128]{1,0:T(4,128)S(1)}, f32[4,128]{1,0:T(4,128)S(1)}, f32[4,128,128]{2,1,0:T(8,128)S(1)}, s32[16]{0:T(128)S(1)}, /*index=5*/s...) while((s32[]{:T(128)}, f32[4,128]{1,0:T(4,128)S(1)}, ...), condition=%wide.region_6.7_spmd.clone, body=%wide.region_1.6_spmd.clone.sunk | while | flops 136775296 | bytes 5152051 | solution.py:86
  493.0 3.3 conditional.3
  498.3 3.3 conditional.3
  503.6 3.3 conditional.3
  509.0 3.3 conditional.3
  514.3 3.3 conditional.3
  519.6 3.3 conditional.3
  524.9 3.3 conditional.3
  530.3 3.3 conditional.3
  535.6 3.3 conditional.3
  540.9 3.3 conditional.3
  551.6 3.3 conditional.3
  562.2 3.3 conditional.3
  572.9 3.3 conditional.3
  (236 shorter events, 93.6 us)
Async XLA Ops:
  13.4 16.4 %copy-start.5 = (bf16[128,512]{1,0:T(8,128)(2,1)S(1)}, bf16[128,512]{1,0:T(8,128)(2,1)}, u32[]{:S(2)}) copy-start(bf16[128,512]{1,0:T(8,128)(2,1)} %param.14) | copy-start | bytes 393220
  13.4 18.9 %copy-start.1 = (bf16[512,512]{1,0:T(8,128)(2,1)S(1)}, bf16[512,512]{1,0:T(8,128)(2,1)}, u32[]{:S(2)}) copy-start(bf16[512,512]{1,0:T(8,128)(2,1)} %param.16) | copy-start | bytes 1572868
  13.4 19.0 %copy-start.6 = (bf16[128,512]{1,0:T(8,128)(2,1)S(1)}, bf16[128,512]{1,0:T(8,128)(2,1)}, u32[]{:S(2)}) copy-start(bf16[128,512]{1,0:T(8,128)(2,1)} %param.17) | copy-start | bytes 393220
  13.4 20.1 %copy-start.7 = (bf16[128,512]{1,0:T(8,128)(2,1)S(1)}, bf16[128,512]{1,0:T(8,128)(2,1)}, u32[]{:S(2)}) copy-start(bf16[128,512]{1,0:T(8,128)(2,1)} %param.11) | copy-start | bytes 393220
  13.5 20.3 %copy-start.2 = (bf16[512,512]{1,0:T(8,128)(2,1)S(1)}, bf16[512,512]{1,0:T(8,128)(2,1)}, u32[]{:S(2)}) copy-start(bf16[512,512]{1,0:T(8,128)(2,1)} %param.15) | copy-start | bytes 1572868
  13.5 415.5 %all-to-all-start = ((bf16[64,128,512]{1,2,0:T(8,128)(2,1)}), bf16[64,128,512]{1,2,0:T(8,128)(2,1)}, u32[]{:S(2)}, u32[]{:S(2)}) async-start(bf16[64,128,512]{1,2,0:T(8,128)(2,1)} %stack.2), calls=%async_computation | async-start | bytes 16777216 | tf_op jit(solution)/shard_map/all_to_all | solution.py:59
  29.1 440.5 %all-gather.2.cloned.1.call-start = ((), (), s32[]{:S(2)}) async-start(), calls=%async_computation.1 | async-start | bytes 8519680 | tf_op jit(solution)/shard_map/all_gather | solution.py:61
  29.8 178.3 %collective-permute-start = (bf16[63,512]{1,0:T(8,128)(2,1)S(1)}, bf16[63,512]{1,0:T(8,128)(2,1)S(1)}, u32[]{:S(2)}, u32[]{:S(2)}) collective-permute-start(bf16[63,512]{1,0:T(8,128)(2,1)S(1)} %slice.13), channel_id=1, source_target_pairs={{8,0},{16,8},{24,16},{32,24},{40,32},{48,40},{56,48},{64,56},{72,6... | collective-permute-start | bytes 193544 | tf_op jit(solution)/shard_map/ppermute | solution.py:14
  32.8 180.5 %copy-start.3 = (f32[2,4,64,256]{3,2,1,0:T(8,128)}, f32[2,4,64,256]{3,2,1,0:T(8,128)S(1)}, u32[]{:S(2)}) copy-start(f32[2,4,64,256]{3,2,1,0:T(8,128)S(1)} %fusion.34) | copy-start | bytes 1572868
  208.2 4.4 copy-start
  209.9 2.7 copy-start.4
  221.2 206.3 %collective-permute-start.1 = (bf16[63,512]{1,0:T(8,128)(2,1)}, bf16[63,512]{1,0:T(8,128)(2,1)}, u32[]{:S(2)}, u32[]{:S(2)}) collective-permute-start(bf16[63,512]{1,0:T(8,128)(2,1)} %slice.16), channel_id=1, source_target_pairs={{0,8},{8,16},{16,24},{24,32},{32,40},{40,48},{48,56},{56,64},{64,7... | collective-permute-start | bytes 193544 | tf_op jit(solution)/shard_map/ppermute | solution.py:14
Sparse Core Ops, SparseCore 0:
  34.4 381.5 all-gather.1
